TPU v7x, 32 devices: a whole 2x2x4 slice. The times are simulated.
32 devices in a mesh: grp: 2 (over y), frame: 4 (over x, core), coil: 4 (over z).
Axes of the slice: x: 2, y: 2, z: 4, core: 2. Of those that a mesh axis runs over, the one named last changes fastest.
Arguments:
- images: bfloat16 [8, 2, 384, 384], P(('grp', 'frame')), parts along dimension 0, may hold values from -6 to 6
- coil_maps: bfloat16 [8, 2, 384, 384], P(('grp', 'coil')), parts along dimension 0, may hold values from -3 to 3
- kspace_data: float32 [8, 4, 2, 6, 128], P(('grp', 'frame'), 'coil'), parts along dimension 0, may hold values from -6 to 6
- spoke_angle: int32 [8, 6], P(('grp', 'frame')), parts along dimension 0, may hold values from 0 to 15
- band_row: int32 [8, 6], P(('grp', 'frame')), parts along dimension 0, may hold values from 0 to 256
- band_col: int32 [8, 6], P(('grp', 'frame')), parts along dimension 0, may hold values from 0 to 256
- kernel_rows: bfloat16 [16, 128, 128], replicated, may hold values from -0.5 to 0.5
- kernel_cols: bfloat16 [16, 128, 128], replicated, may hold values from -0.5 to 0.5
Outputs:
- updated: float32 [8, 2, 384, 384], P(('grp', 'frame')), parts along dimension 0
There are 2 independent parts, one for each index of `grp`. A program takes and returns all parts, laid end to end along the dimension named above; an argument that names none is the same for every part. Nothing has to cross between parts.
All inputs are finite; a program needn't handle non-finite values.
Results may differ from a plain program's by a relative error of at most 0.0014.
Values may be sent and summed in bfloat16 or wider, within the bound.
No kernel may reach another device: no remote copies, remote signals or barrier semaphores. Data moves between devices by JAX's collectives and lax.ppermute only.
A program may use at most 64 MiB of HBM per device.

v0:
```python
import math
import jax
import jax.numpy as jnp
from jax import lax
from jax.sharding import PartitionSpec as P

SMOOTHING = 0.05
STEP_SIZE = 1.0
TV_WEIGHT = 0.2


def padded(cells, sides, width):
    for axis, dim in sides:
        count = lax.axis_size(axis)
        ends = count - 1
        head = lax.slice_in_dim(cells, 0, width, axis=dim)
        tail = lax.slice_in_dim(cells, cells.shape[dim] - width, cells.shape[dim], axis=dim)
        cells = jnp.concatenate(
            [
                lax.ppermute(tail, axis, [(i, (i + 1) % count) for i in range(ends)]),
                cells,
                lax.ppermute(head, axis, [((i + 1) % count, i) for i in range(ends)]),
            ],
            axis=dim,
        )
    return cells


def transform_table(extent):
    indices = jnp.arange(extent, dtype=jnp.int32)
    phases = indices[:, None] * indices[None, :] % extent
    angle_values = 2.0 * math.pi / extent * phases.astype(jnp.float32)
    scaling = 1.0 / math.sqrt(extent)
    return jnp.stack([jnp.cos(angle_values) * scaling, jnp.sin(angle_values) * scaling]).astype(
        jnp.bfloat16
    )


def combine_parts(products, direction):
    real_part = products[0, 0] + direction * products[1, 1]
    imaginary = products[0, 1] - direction * products[1, 0]
    return jnp.stack([real_part, imaginary])


def apply_update(own_rows, extended, data_grad, first_frame, frame_total):
    widened = extended.astype(jnp.float32)
    change = widened[1:] - widened[:-1]
    position = first_frame - 1 + jnp.arange(change.shape[0], dtype=jnp.int32)
    inside = ((position >= 0) & (position <= frame_total - 2)).astype(jnp.float32)
    normed = inside[:, None, None, None] * (
        change / jnp.sqrt(jnp.sum(change * change, axis=1, keepdims=True) + SMOOTHING)
    )
    tv_grad = normed[:-1] - normed[1:]
    return own_rows.astype(jnp.float32) - STEP_SIZE * (data_grad + TV_WEIGHT * tv_grad)


def rotated(block, coil_count, shift):
    return lax.ppermute(block, "coil", [(i, (i + shift) % coil_count) for i in range(coil_count)])


def exchange_rows(coil_map, rows, coil_count, coil_index):
    received = [lax.dynamic_slice_in_dim(coil_map, coil_index * rows, rows, axis=1)]
    for shift in range(1, coil_count):
        target = (coil_index + shift) % coil_count
        block = lax.dynamic_slice_in_dim(coil_map, target * rows, rows, axis=1)
        received.append(rotated(block, coil_count, shift))
    return jnp.stack(received)


def selector(first_index, extent, patch_side):
    positions = jnp.arange(extent, dtype=jnp.int32)
    offsets = jnp.arange(patch_side, dtype=jnp.int32)
    wanted = first_index[:, None, None] + offsets[None, None, :]
    return (positions[None, :, None] == wanted).astype(jnp.bfloat16)


def pick_kernels(kernels, angle_ids):
    choice = angle_ids[:, None] == jnp.arange(kernels.shape[0], dtype=jnp.int32)[None, :]
    flat = kernels.reshape(kernels.shape[0], -1)
    picked = jnp.dot(choice.astype(kernels.dtype), flat, preferred_element_type=jnp.float32)
    return picked.astype(kernels.dtype).reshape((angle_ids.shape[0],) + kernels.shape[1:])


def forward_residual(
    transform, frame_image, coil_map, measured, row_select, col_select, row_w, col_w
):
    map_planes = coil_map.astype(jnp.float32)
    image_planes = frame_image.astype(jnp.float32)
    coil_image = jnp.stack(
        [
            map_planes[0] * image_planes[0] - map_planes[1] * image_planes[1],
            map_planes[0] * image_planes[1] + map_planes[1] * image_planes[0],
        ]
    ).astype(jnp.bfloat16)
    products = jnp.einsum(
        "aij,bjk->abik", transform, coil_image, preferred_element_type=jnp.float32
    )
    half_done = combine_parts(products, 1.0).astype(jnp.bfloat16)
    products = jnp.einsum("bij,ajk->abik", half_done, transform, preferred_element_type=jnp.float32)
    kspace = combine_parts(products, 1.0).astype(jnp.bfloat16)
    picked_rows = jnp.einsum(
        "gir,pik->pgrk", row_select, kspace, preferred_element_type=jnp.float32
    ).astype(jnp.bfloat16)
    patches = jnp.einsum(
        "pgrk,gkq->pgrq", picked_rows, col_select, preferred_element_type=jnp.float32
    ).astype(jnp.bfloat16)
    contracted = jnp.einsum("pgrq,gjq->pgrj", patches, col_w, preferred_element_type=jnp.float32)
    predicted = jnp.sum(contracted * row_w.astype(jnp.float32)[None], axis=2)
    return predicted - measured


def backward_rows(transform, residuals, map_rows, row_select, col_select, row_w, col_w, coil_index):
    rows = map_rows.shape[2]
    spread = (row_w.astype(jnp.float32)[None, None] * residuals[:, :, :, None, :]).astype(
        jnp.bfloat16
    )
    spread_back = jnp.einsum("cpgrj,gjq->cpgrq", spread, col_w, preferred_element_type=jnp.float32)
    placed = jnp.einsum(
        "cpgrq,gkq->cpgrk",
        spread_back.astype(jnp.bfloat16),
        col_select,
        preferred_element_type=jnp.float32,
    ).astype(jnp.bfloat16)
    row_table = lax.dynamic_slice_in_dim(transform, coil_index * rows, rows, axis=1)
    table_at = jnp.einsum(
        "aij,gjr->aigr", row_table, row_select, preferred_element_type=jnp.float32
    ).astype(jnp.bfloat16)
    products = jnp.einsum("aigr,cbgrk->abcik", table_at, placed, preferred_element_type=jnp.float32)
    half_back = combine_parts(products, -1.0).astype(jnp.bfloat16)
    products = jnp.einsum(
        "bcij,ajk->abcik", half_back, transform, preferred_element_type=jnp.float32
    )
    coil_back = combine_parts(products, -1.0)
    maps = map_rows.astype(jnp.float32)
    real_part = jnp.sum(maps[:, 0] * coil_back[0] + maps[:, 1] * coil_back[1], axis=0)
    imaginary = jnp.sum(maps[:, 0] * coil_back[1] - maps[:, 1] * coil_back[0], axis=0)
    return jnp.stack([real_part, imaginary])


def local(
    images, coil_maps, kspace_data, spoke_angle, band_row, band_col, kernel_rows, kernel_cols
):
    frame_count = images.shape[0]
    extent = images.shape[-1]
    patch_side = kernel_cols.shape[-1]
    coil_count = lax.axis_size("coil")
    coil_index = lax.axis_index("coil")
    rows = extent // coil_count
    transform = transform_table(extent)
    map_rows = exchange_rows(coil_maps[0], rows, coil_count, coil_index)
    first_frame = lax.axis_index("frame") * frame_count
    frame_total = lax.axis_size("frame") * frame_count
    extended = padded(images, (("frame", 0),), 1)
    row_w = pick_kernels(kernel_rows, spoke_angle[0])
    col_w = pick_kernels(kernel_cols, spoke_angle[0])
    row_select = selector(band_row[0], extent, patch_side)
    col_select = selector(band_col[0], extent, patch_side)
    residual = forward_residual(
        transform, images[0], coil_maps[0], kspace_data[0, 0], row_select, col_select, row_w, col_w
    )
    residuals = jnp.stack(
        [residual] + [rotated(residual, coil_count, shift) for shift in range(1, coil_count)]
    )
    grad_rows = backward_rows(
        transform, residuals, map_rows, row_select, col_select, row_w, col_w, coil_index
    )
    data_grad = lax.all_gather(grad_rows.astype(jnp.bfloat16), "coil", axis=1, tiled=True)
    data_grad = data_grad.astype(jnp.float32)[None]
    return apply_update(images, extended, data_grad, first_frame, frame_total)


def solution(mesh):
    in_specs = (
        P(("grp", "frame"), None, None, None),
        P(("grp", "coil"), None, None, None),
        P(("grp", "frame"), "coil", None, None, None),
        P(("grp", "frame"), None),
        P(("grp", "frame"), None),
        P(("grp", "frame"), None),
        P(),
        P(),
    )
    out_specs = P(("grp", "frame"), None, None, None)
    return jax.shard_map(local, mesh=mesh, in_specs=in_specs, out_specs=out_specs, check_vma=False)
```

profile of v0, /device:TPU:0, one launch (start us, length us, event | category | flops | bytes accessed | tf_op | source)
XLA Modules:
  0.0 64.8 jit_solution(3181471237074977384)
XLA Ops:
  0.0 1.4 %copy.24 = bf16[1,2,384,384]{2,3,1,0:T(8,128)(2,1)S(1)} copy(bf16[1,2,384,384]{3,2,1,0:T(8,128)(2,1)} %param.8) | data formatting | bytes 1179648 | tf_op args[0]
  1.4 1.3 %collective-permute-start.7 = (bf16[1,2,384,384]{2,3,1,0:T(8,128)(2,1)S(1)}, bf16[1,2,384,384]{2,3,1,0:T(8,128)(2,1)}, u32[]{:S(2)}, u32[]{:S(2)}) collective-permute-start(bf16[1,2,384,384]{2,3,1,0:T(8,128)(2,1)S(1)} %copy.24), channel_id=1, source_target_pairs={{4,0},{8,4},{12,8},{5,1},{9,5},{13,9},{6,2},{10,6},{14,10},{7,3},{... | collective-permute-start | bytes 1769480 | tf_op jit(solution)/shard_map/ppermute | solution.py:22
  2.7 3.9 %collective-permute-start.6 = (bf16[1,2,384,384]{2,3,1,0:T(8,128)(2,1)S(1)}, bf16[1,2,384,384]{2,3,1,0:T(8,128)(2,1)}, u32[]{:S(2)}, u32[]{:S(2)}) collective-permute-start(bf16[1,2,384,384]{2,3,1,0:T(8,128)(2,1)S(1)} %copy.24), channel_id=1, source_target_pairs={{0,4},{4,8},{8,12},{1,5},{5,9},{9,13},{2,6},{6,10},{10,14},{3,7},{... | collective-permute-start | bytes 1769480 | tf_op jit(solution)/shard_map/ppermute | solution.py:20
  6.6 2.6 %multiply_convert_fusion.1 = (bf16[1,384,384]{2,1,0:T(8,128)(2,1)S(1)}, bf16[1,384,384]{2,1,0:T(8,128)(2,1)S(1)}) fusion(), kind=kLoop, calls=%fused_computation.99 | loop fusion | flops 1916928 | bytes 589824 | tf_op jit(solution)/shard_map/convert.23
  9.9 0.8 %convolution_bitcast_fusion.2 = f32[2,2,384,384]{2,3,0,1:T(8,128)S(1)} fusion(bf16[1,384,384]{1,2,0:T(8,128)(2,1)S(1)} %get-tuple-element.10, bf16[1,384,384]{1,2,0:T(8,128)(2,1)S(1)} %get-tuple-element.9, bf16[1,384,384]{2,1,0:T(8,128)(2,1)S(1)} %get-tuple-element.14, bf16[1,384,384]{2,1,0:T(8,128)(2,1)S(1)} %get-tuple-element.15), kind=kOutput, calls=%fused_computation.17 | convolution fusion | flops 455344128 | bytes 3538944 | tf_op jit(solution)/shard_map/aij,bjk->abik/dot_general | solution.py:95
  11.8 1.1 %fusion.33 = bf16[1,6,128,128]{3,1,2,0:T(8,128)(2,1)} fusion(bf16[2,8,128,128]{3,2,1,0:T(8,128)(2,1)S(1)} %bitcast.236, s32[6]{0:T(128)S(1)} %bitcast.243), kind=kOutput, calls=%fused_computation.42 | convolution fusion | flops 3244128 | bytes 720920 | tf_op jit(solution)/shard_map/dot_general | solution.py:80
  13.3 0.8 %copy.104 = f32[1,6,128,128]{3,2,1,0:T(8,128)} copy(f32[1,6,128,128]{3,1,2,0:T(8,128)S(1)} %fusion.14) | data formatting | bytes 786432
  14.1 0.8 %convolution_bitcast_fusion.1 = f32[2,2,384,384]{2,3,1,0:T(8,128)S(1)} fusion(bf16[1,384,384]{1,2,0:T(8,128)(2,1)S(1)} %fusion.81, bf16[1,384,384]{1,2,0:T(8,128)(2,1)S(1)} %fusion.80, bf16[1,384,384]{2,1,0:T(8,128)(2,1)S(1)} %get-tuple-element.14, bf16[1,384,384]{2,1,0:T(8,128)(2,1)S(1)} %get-tuple-element.15), kind=kOutput, calls=%fused_computation.16 | convolution fusion | flops 455344128 | bytes 3538944 | tf_op jit(solution)/shard_map/bij,ajk->abik/dot_general | solution.py:99
  15.0 0.8 %fusion.28 = bf16[2,384,6,128]{3,1,2,0:T(8,128)(2,1)S(1)} fusion(bf16[1,384,384]{1,2,0:T(8,128)(2,1)S(1)} %get-tuple-element.8, bf16[1,384,384]{1,2,0:T(8,128)(2,1)S(1)} %get-tuple-element.7, s32[6,128]{1,0:T(8,128)S(1)} %iota_add_fusion), kind=kOutput, calls=%fused_computation.40 | convolution fusion | flops 454459392 | bytes 1772544 | tf_op jit(solution)/shard_map/gir,pik->pgrk/dot_general | solution.py:101
  15.9 0.8 %copy.102 = bf16[2,384,6,128]{3,2,1,0:T(8,128)(2,1)S(1)} copy(bf16[2,384,6,128]{3,1,2,0:T(8,128)(2,1)S(1)} %fusion.28) | data formatting | bytes 2359296 | tf_op jit(solution)/shard_map/gir,pik->pgrk/dot_general | solution.py:101
  16.7 1.9 %fusion.15 = f32[2,6,128]{2,0,1:T(2,128)S(1)} fusion(bf16[2,6,128,384]{2,1,3,0:T(8,128)(2,1)S(1)} %bitcast.233, s32[6,128]{1,0:T(8,128)S(1)} %iota_add_fusion.1, f32[6,128,128]{2,1,0:T(8,128)} %bitcast.234, bf16[1,6,128,128]{3,1,2,0:T(8,128)(2,1)} %fusion.33), kind=kOutput, calls=%fused_computation.27 | convolution fusion | flops 202209792 | bytes 1778688 | tf_op jit(solution)/shard_map/pgrq,gjq->pgrj/dot_general | solution.py:107
  18.6 5.1 %collective-permute-start.5 = (f32[2,6,128]{2,0,1:T(2,128)S(1)}, f32[2,6,128]{2,0,1:T(2,128)S(1)}, u32[]{:S(2)}, u32[]{:S(2)}) collective-permute-start(f32[2,6,128]{2,0,1:T(2,128)S(1)} %bitcast_subtract_fusion), channel_id=1, source_target_pairs={{0,3},{1,0},{2,1},{3,2},{4,7},{5,4},{6,5},{7,6},{8,11},{9,8},{10,9... | collective-permute-start | bytes 18440 | tf_op jit(solution)/shard_map/ppermute | solution.py:58
  23.7 1.0 %collective-permute-start.3 = (f32[2,6,128]{2,0,1:T(2,128)S(1)}, f32[2,6,128]{2,0,1:T(2,128)S(1)}, u32[]{:S(2)}, u32[]{:S(2)}) collective-permute-start(f32[2,6,128]{2,0,1:T(2,128)S(1)} %bitcast_subtract_fusion), channel_id=1, source_target_pairs={{0,1},{1,2},{2,3},{3,0},{4,5},{5,6},{6,7},{7,4},{8,9},{9,10},{10,1... | collective-permute-start | bytes 18440 | tf_op jit(solution)/shard_map/ppermute | solution.py:58
  24.7 1.1 %fusion.30 = bf16[2,96,6,128,1,1]{3,1,2,0,5,4:T(8,128)(2,1)} fusion(s32[6,128]{1,0:T(8,128)S(1)} %iota_add_fusion, s32[]{:T(128)S(6)} %select_n.47, bf16[1,384,384]{2,1,0:T(8,128)(2,1)S(1)} %get-tuple-element.15, bf16[1,384,384]{2,1,0:T(8,128)(2,1)S(1)} %get-tuple-element.14), kind=kOutput, calls=%fused_computation.41 | convolution fusion | flops 113983488 | bytes 887812 | tf_op jit(solution)/shard_map/aij,gjr->aigr/dot_general | solution.py:125
  27.3 2.5 %collective-permute-start = (bf16[2,96,384]{2,1,0:T(8,128)(2,1)}, bf16[2,96,384]{2,1,0:T(8,128)(2,1)}, u32[]{:S(2)}, u32[]{:S(2)}) collective-permute-start(bf16[2,96,384]{2,1,0:T(8,128)(2,1)} %get-tuple-element.11), channel_id=1, source_target_pairs={{0,1},{1,2},{2,3},{3,0},{4,5},{5,6},{6,7},{7,4},{8,9},{9,10},{10,1... | collective-permute-start | bytes 442376 | tf_op jit(solution)/shard_map/ppermute | solution.py:58
  29.8 0.9 %collective-permute-start.1 = (bf16[2,96,384]{2,1,0:T(8,128)(2,1)}, bf16[2,96,384]{2,1,0:T(8,128)(2,1)}, u32[]{:S(2)}, u32[]{:S(2)}) collective-permute-start(bf16[2,96,384]{2,1,0:T(8,128)(2,1)} %get-tuple-element.12), channel_id=1, source_target_pairs={{0,2},{1,3},{2,0},{3,1},{4,6},{5,7},{6,4},{7,5},{8,10},{9,11},{10,... | collective-permute-start | bytes 442376 | tf_op jit(solution)/shard_map/ppermute | solution.py:58
  30.7 1.6 %collective-permute-start.2 = (bf16[2,96,384]{2,1,0:T(8,128)(2,1)}, bf16[2,96,384]{2,1,0:T(8,128)(2,1)}, u32[]{:S(2)}, u32[]{:S(2)}) collective-permute-start(bf16[2,96,384]{2,1,0:T(8,128)(2,1)} %get-tuple-element.13), channel_id=1, source_target_pairs={{0,3},{1,0},{2,1},{3,2},{4,7},{5,4},{6,5},{7,6},{8,11},{9,8},{10,9... | collective-permute-start | bytes 442376 | tf_op jit(solution)/shard_map/ppermute | solution.py:58
  33.0 2.8 %copy.103 = bf16[6,128,4,2,128]{4,3,2,1,0:T(2,128)(2,1)} copy(bf16[6,128,4,2,128]{4,1,3,2,0:T(8,128)(2,1)S(1)} %convolution_convert_fusion.2) | data formatting | bytes 3145728
  35.7 3.8 %fusion.6 = f32[2,2,4,96,384]{4,3,0,1,2:T(8,128)S(1)} fusion(bf16[2,96,6,128,1,1]{3,1,2,0,5,4:T(8,128)(2,1)} %fusion.30, bf16[4,2,6,128,128]{3,1,0,4,2:T(2,128)(2,1)} %bitcast.232, s32[6,128]{1,0:T(8,128)S(1)} %iota_add_fusion.1), kind=kOutput, calls=%fused_computation.13 | convolution fusion | flops 1512603648 | bytes 4230144 | tf_op jit(solution)/shard_map/aigr,cbgrk->abcik/dot_general | solution.py:128
  41.1 1.2 %maximum_convert_fusion.1 = f32[4,2,96,384]{3,2,0,1:T(8,128)S(1)} fusion(bf16[1,2,96,384]{3,2,0,1:T(8,128)(2,1)} %bitcast.6, bf16[1,2,96,384]{3,2,0,1:T(8,128)(2,1)} %bitcast.4, bf16[1,2,96,384]{3,2,0,1:T(8,128)(2,1)} %bitcast.2, bf16[1,2,96,384]{3,2,0,1:T(8,128)(2,1)S(1)} %copy-done.3), kind=kLoop, calls=%fused_computation.75 | loop fusion | flops 1179648 | bytes 1769472 | tf_op jit(solution)/shard_map/convert_element_type | solution.py:134
  42.7 17.0 %all_gather.3 = bf16[2,384,384]{2,0,1:T(2,128)(2,1)S(1)} all-gather(bf16[2,96,384]{2,0,1:T(2,128)(2,1)S(1)} %copy.35), channel_id=1, replica_groups=mesh['grp'=2,'frame'=4,'coil'=4] {'coil'}, dimensions={1}, use_global_device_ids=true | all-gather | bytes 737280 | tf_op jit(solution)/shard_map/all_gather | solution.py:167
  59.7 1.0 %copy.36 = bf16[2,384,384]{1,2,0:T(8,128)(2,1)S(1)} copy(bf16[2,384,384]{2,0,1:T(2,128)(2,1)S(1)} %all_gather.3) | data formatting | bytes 1179648 | tf_op jit(solution)/shard_map/all_gather | solution.py:167
  60.7 1.5 %maximum_convert_fusion = f32[3,2,384,384]{2,3,1,0:T(8,128)S(1)} fusion(bf16[1,2,384,384]{2,3,1,0:T(8,128)(2,1)} %collective-permute-done.7, bf16[1,2,384,384]{2,3,1,0:T(8,128)(2,1)S(1)} %copy.24, bf16[1,2,384,384]{2,3,1,0:T(8,128)(2,1)} %collective-permute-done.6), kind=kLoop, calls=%fused_computation.12 | loop fusion | flops 2654208 | bytes 5308416 | tf_op jit(solution)/shard_map/convert_element_type | solution.py:46
  63.4 1.4 %copy.40 = f32[1,2,384,384]{3,2,1,0:T(8,128)} copy(f32[1,2,384,384]{2,3,1,0:T(8,128)S(1)} %fusion.19) | data formatting | bytes 2359296 | tf_op jit(solution)/shard_map/sub | solution.py:54
  (57 shorter events, 7.4 us)
Async XLA Ops:
  0.0 9.3 %copy-start = (bf16[1,2,384,384]{3,2,1,0:T(8,128)(2,1)S(1)}, bf16[1,2,384,384]{3,2,1,0:T(8,128)(2,1)}, u32[]{:S(2)}) copy-start(bf16[1,2,384,384]{3,2,1,0:T(8,128)(2,1)} %param.9) | copy-start | bytes 1769476
  1.4 59.3 %collective-permute-start.7 = (bf16[1,2,384,384]{2,3,1,0:T(8,128)(2,1)S(1)}, bf16[1,2,384,384]{2,3,1,0:T(8,128)(2,1)}, u32[]{:S(2)}, u32[]{:S(2)}) collective-permute-start(bf16[1,2,384,384]{2,3,1,0:T(8,128)(2,1)S(1)} %copy.24), channel_id=1, source_target_pairs={{4,0},{8,4},{12,8},{5,1},{9,5},{13,9},{6,2},{10,6},{14,10},{7,3},{... | collective-permute-start | bytes 1769480 | tf_op jit(solution)/shard_map/ppermute | solution.py:22
  2.7 58.0 %collective-permute-start.6 = (bf16[1,2,384,384]{2,3,1,0:T(8,128)(2,1)S(1)}, bf16[1,2,384,384]{2,3,1,0:T(8,128)(2,1)}, u32[]{:S(2)}, u32[]{:S(2)}) collective-permute-start(bf16[1,2,384,384]{2,3,1,0:T(8,128)(2,1)S(1)} %copy.24), channel_id=1, source_target_pairs={{0,4},{4,8},{8,12},{1,5},{5,9},{9,13},{2,6},{6,10},{10,14},{3,7},{... | collective-permute-start | bytes 1769480 | tf_op jit(solution)/shard_map/ppermute | solution.py:20
  10.7 0.7 %copy-start.8 = (s32[1,6]{1,0:T(1,128)S(1)}, s32[1,6]{1,0:T(1,128)}, u32[]{:S(2)}) copy-start(s32[1,6]{1,0:T(1,128)} %param.12) | copy-start | bytes 76
  10.7 0.7 %copy-start.9 = (s32[1,6]{1,0:T(1,128)S(1)}, s32[1,6]{1,0:T(1,128)}, u32[]{:S(2)}) copy-start(s32[1,6]{1,0:T(1,128)} %param.13) | copy-start | bytes 76
  10.7 1.1 %copy-start.4 = (bf16[16,128,128]{2,1,0:T(8,128)(2,1)S(1)}, bf16[16,128,128]{2,1,0:T(8,128)(2,1)}, u32[]{:S(2)}) copy-start(bf16[16,128,128]{2,1,0:T(8,128)(2,1)} %param.15) | copy-start | bytes 1572868
  10.7 1.0 %copy-start.7 = (s32[1,6]{1,0:T(1,128)S(1)}, s32[1,6]{1,0:T(1,128)}, u32[]{:S(2)}) copy-start(s32[1,6]{1,0:T(1,128)} %param.11) | copy-start | bytes 76
  10.7 2.1 %copy-start.5 = (bf16[16,128,128]{2,1,0:T(8,128)(2,1)S(1)}, bf16[16,128,128]{2,1,0:T(8,128)(2,1)}, u32[]{:S(2)}) copy-start(bf16[16,128,128]{2,1,0:T(8,128)(2,1)} %param.14) | copy-start | bytes 1572868
  16.7 1.9 %copy-start.6 = (f32[1,1,2,6,128]{4,2,3,1,0:T(2,128)S(1)}, f32[1,1,2,6,128]{4,2,3,1,0:T(2,128)}, u32[]{:S(2)}) copy-start(f32[1,1,2,6,128]{4,2,3,1,0:T(2,128)} %param.10) | copy-start | bytes 18436
  18.6 13.8 %copy-start.1 = (f32[1,6,128,128]{3,2,1,0:T(8,128)S(1)}, f32[1,6,128,128]{3,2,1,0:T(8,128)}, u32[]{:S(2)}) copy-start(f32[1,6,128,128]{3,2,1,0:T(8,128)} %copy.104) | copy-start | bytes 1179652
  18.6 13.8 %copy-start.2 = (bf16[1,6,128,128]{3,1,2,0:T(8,128)(2,1)S(1)}, bf16[1,6,128,128]{3,1,2,0:T(8,128)(2,1)}, u32[]{:S(2)}) copy-start(bf16[1,6,128,128]{3,1,2,0:T(8,128)(2,1)} %fusion.33) | copy-start | bytes 589828
  18.6 8.7 %collective-permute-start.5 = (f32[2,6,128]{2,0,1:T(2,128)S(1)}, f32[2,6,128]{2,0,1:T(2,128)S(1)}, u32[]{:S(2)}, u32[]{:S(2)}) collective-permute-start(f32[2,6,128]{2,0,1:T(2,128)S(1)} %bitcast_subtract_fusion), channel_id=1, source_target_pairs={{0,3},{1,0},{2,1},{3,2},{4,7},{5,4},{6,5},{7,6},{8,11},{9,8},{10,9... | collective-permute-start | bytes 18440 | tf_op jit(solution)/shard_map/ppermute | solution.py:58
  23.7 6.1 %collective-permute-start.4 = (f32[2,6,128]{2,0,1:T(2,128)S(1)}, f32[2,6,128]{2,0,1:T(2,128)S(1)}, u32[]{:S(2)}, u32[]{:S(2)}) collective-permute-start(f32[2,6,128]{2,0,1:T(2,128)S(1)} %bitcast_subtract_fusion), channel_id=1, source_target_pairs={{0,2},{1,3},{2,0},{3,1},{4,6},{5,7},{6,4},{7,5},{8,10},{9,11},{10,... | collective-permute-start | bytes 18440 | tf_op jit(solution)/shard_map/ppermute | solution.py:58
  23.7 7.0 %collective-permute-start.3 = (f32[2,6,128]{2,0,1:T(2,128)S(1)}, f32[2,6,128]{2,0,1:T(2,128)S(1)}, u32[]{:S(2)}, u32[]{:S(2)}) collective-permute-start(f32[2,6,128]{2,0,1:T(2,128)S(1)} %bitcast_subtract_fusion), channel_id=1, source_target_pairs={{0,1},{1,2},{2,3},{3,0},{4,5},{5,6},{6,7},{7,4},{8,9},{9,10},{10,1... | collective-permute-start | bytes 18440 | tf_op jit(solution)/shard_map/ppermute | solution.py:58
  27.3 13.2 %collective-permute-start = (bf16[2,96,384]{2,1,0:T(8,128)(2,1)}, bf16[2,96,384]{2,1,0:T(8,128)(2,1)}, u32[]{:S(2)}, u32[]{:S(2)}) collective-permute-start(bf16[2,96,384]{2,1,0:T(8,128)(2,1)} %get-tuple-element.11), channel_id=1, source_target_pairs={{0,1},{1,2},{2,3},{3,0},{4,5},{5,6},{6,7},{7,4},{8,9},{9,10},{10,1... | collective-permute-start | bytes 442376 | tf_op jit(solution)/shard_map/ppermute | solution.py:58
  29.8 11.2 %collective-permute-start.1 = (bf16[2,96,384]{2,1,0:T(8,128)(2,1)}, bf16[2,96,384]{2,1,0:T(8,128)(2,1)}, u32[]{:S(2)}, u32[]{:S(2)}) collective-permute-start(bf16[2,96,384]{2,1,0:T(8,128)(2,1)} %get-tuple-element.12), channel_id=1, source_target_pairs={{0,2},{1,3},{2,0},{3,1},{4,6},{5,7},{6,4},{7,5},{8,10},{9,11},{10,... | collective-permute-start | bytes 442376 | tf_op jit(solution)/shard_map/ppermute | solution.py:58
  30.7 10.3 %collective-permute-start.2 = (bf16[2,96,384]{2,1,0:T(8,128)(2,1)}, bf16[2,96,384]{2,1,0:T(8,128)(2,1)}, u32[]{:S(2)}, u32[]{:S(2)}) collective-permute-start(bf16[2,96,384]{2,1,0:T(8,128)(2,1)} %get-tuple-element.13), channel_id=1, source_target_pairs={{0,3},{1,0},{2,1},{3,2},{4,7},{5,4},{6,5},{7,6},{8,11},{9,8},{10,9... | collective-permute-start | bytes 442376 | tf_op jit(solution)/shard_map/ppermute | solution.py:58
  39.7 1.4 %copy-start.3 = (bf16[1,2,96,384]{3,2,0,1:T(8,128)(2,1)S(1)}, bf16[1,2,96,384]{3,2,0,1:T(8,128)(2,1)}, u32[]{:S(2)}) copy-start(bf16[1,2,96,384]{3,2,0,1:T(8,128)(2,1)} %constant_dynamic-slice_fusion) | copy-start | bytes 442372
where the time goes:
time: 65.1 us; the launch traced here: 64.8 us
  blocking collectives  17 us (26%)
  starting transfers between devices  16.3 us (25%)
  matrix products  12.1 us (19%)
  local copies, waits for them, and re-layouts  10.9 us (17%)
  other arithmetic  7.57 us (12%)
    all_gather x1, blocking collectives, local(): lax.all_gather(grad_rows.astype(jnp.bfloat16), 'coil', axis=1, tiled=True)  17 us
    ppermute x6, starting transfers between devices, rotated(): lax.ppermute(block, 'coil', [(i, (i + shift) % coil_count) for i in range...  11.1 us
    unnamed x24, local copies, waits for them, and re-layouts  6.13 us
    ppermute x1, starting transfers between devices, padded(): lax.ppermute(tail, axis, [(i, (i + 1) % count) for i in range(ends)])  3.87 us
    dot_general x1, matrix products, backward_rows(): jnp.einsum('aigr,cbgrk->abcik', table_at, placed, preferred_element_type=...  3.78 us
    another operation x1, other arithmetic  2.58 us
    dot_general x1, matrix products, forward_residual(): jnp.einsum('pgrq,gjq->pgrj', patches, col_w, preferred_element_type=jnp.f...  1.86 us
    convert_element_type x1, other arithmetic, apply_update(): widened = extended.astype(jnp.float32)  1.52 us
  transfers between devices with their start and end apart: 8, of which 1 were waited for; matrix products, arithmetic and copies ran while one was open for 37% of the time, Pallas kernels for 0%

commit v1 on v0

--- a/solution.py
+++ b/solution.py
@@ -7,6 +7,12 @@
 SMOOTHING = 0.05
 STEP_SIZE = 1.0
 TV_WEIGHT = 0.2
+
+
+def joined_along(blocks, dim):
+    blocks = jnp.moveaxis(blocks, 0, dim)
+    dims = blocks.shape
+    return blocks.reshape(*dims[:dim], dims[dim] * dims[dim + 1], *dims[dim + 2 :])
 
 
 def padded(cells, sides, width):
@@ -164,7 +170,20 @@
     grad_rows = backward_rows(
         transform, residuals, map_rows, row_select, col_select, row_w, col_w, coil_index
     )
-    data_grad = lax.all_gather(grad_rows.astype(jnp.bfloat16), "coil", axis=1, tiled=True)
+    shard = grad_rows.astype(jnp.bfloat16)
+    length = lax.axis_size("coil")
+    pairs = [(i_2, (i_2 + 1) % length) for i_2 in range(length)]
+    back = [(b, a) for a, b in pairs]
+    lower, upper = ([], [])
+    for hop in range(length - 1):
+        if hop % 2 == 0:
+            lower.append(lax.ppermute(lower[-1] if lower else shard, "coil", pairs))
+        else:
+            upper.append(lax.ppermute(upper[-1] if upper else shard, "coil", back))
+    blocks = jnp.stack([*lower[::-1], shard, *upper])
+    shift_2 = lax.axis_index("coil") - len(lower)
+    blocks = blocks[(jnp.arange(length) - shift_2) % length]
+    data_grad = joined_along(blocks, 1)
     data_grad = data_grad.astype(jnp.float32)[None]
     return apply_update(images, extended, data_grad, first_frame, frame_total)
 

time: 65.1 us -> 59.5 us (0.914)
  blocking collectives: 17 us -> 0 us
  waiting for transfers between devices: 0.62 us -> 7.96 us
  starting transfers between devices: 16.3 us -> 20.3 us
    all_gather x1 -> x0, blocking collectives: 17 us -> none  [local(): lax.all_gather(grad_rows.astype(jnp.bfloat16), 'coil', axis=1, tiled=True)]
    ppermute x0 -> x3, waiting for transfers between devices: none -> 7.94 us  [the longest x1 4.04 us: local(): upper.append(lax.ppermute(upper[-1] if upper else shard, 'coil', back))]
    ppermute x0 -> x3, starting transfers between devices: none -> 4.16 us  [the longest x2 2.31 us: local(): lower.append(lax.ppermute(lower[-1] if lower else shard, 'coil', pairs))]
    dot_general x1, local copies, waits for them, and re-layouts: 0.81 us -> 1.98 us  [forward_residual(): jnp.einsum('gir,pik->pgrk', row_select, kspace, preferred_element_type=jn...]
    all_gather x1 -> x0, local copies, waits for them, and re-layouts: 0.99 us -> none  [local(): lax.all_gather(grad_rows.astype(jnp.bfloat16), 'coil', axis=1, tiled=True)]
    unnamed x24 -> x20, local copies, waits for them, and re-layouts: 6.13 us -> 5.4 us
    dot_general x2, matrix products: 1.52 us -> 0.8 us  [pick_kernels(): jnp.dot(choice.astype(kernels.dtype), flat, preferred_element_type=jnp.fl...]
    gather x0 -> x1, local copies, waits for them, and re-layouts: none -> 0.68 us  [local(): blocks = blocks[(jnp.arange(length) - shift_2) % length]]
  transfers between devices with their start and end apart: 8 -> 11, of which waited for: 1 -> 2; matrix products, arithmetic and copies ran while one was open for 37% -> 20% of each run, Pallas kernels for 0% -> 0%
where the time goes in v1:
time: 59.5 us; the launch traced here: 59.2 us
  starting transfers between devices  20.3 us (34%)
  matrix products  11.7 us (20%)
  local copies, waits for them, and re-layouts  11.3 us (19%)
  waiting for transfers between devices  7.96 us (13%)
  other arithmetic  7.53 us (13%)
    ppermute x6, starting transfers between devices, rotated(): lax.ppermute(block, 'coil', [(i, (i + shift) % coil_count) for i in range...  11 us
    unnamed x20, local copies, waits for them, and re-layouts  5.4 us
    ppermute x1, waiting for transfers between devices, local(): upper.append(lax.ppermute(upper[-1] if upper else shard, 'coil', back))  4.04 us
    ppermute x2, waiting for transfers between devices, local(): lower.append(lax.ppermute(lower[-1] if lower else shard, 'coil', pairs))  3.9 us
    ppermute x1, starting transfers between devices, padded(): lax.ppermute(tail, axis, [(i, (i + 1) % count) for i in range(ends)])  3.86 us
    dot_general x1, matrix products, backward_rows(): jnp.einsum('aigr,cbgrk->abcik', table_at, placed, preferred_element_type=...  3.78 us
    another operation x1, other arithmetic  2.58 us
    ppermute x2, starting transfers between devices, local(): lower.append(lax.ppermute(lower[-1] if lower else shard, 'coil', pairs))  2.31 us
  transfers between devices with their start and end apart: 11, of which 2 were waited for; matrix products, arithmetic and copies ran while one was open for 20% of the time, Pallas kernels for 0%

profile of v1, /device:TPU:0, one launch (start us, length us, event | category | flops | bytes accessed | tf_op | source)
XLA Modules:
  0.0 59.2 jit_solution(11335108479239949951)
XLA Ops:
  0.0 2.6 %multiply_convert_fusion.1 = (bf16[1,384,384]{2,1,0:T(8,128)(2,1)S(1)}, bf16[1,384,384]{2,1,0:T(8,128)(2,1)S(1)}) fusion(), kind=kLoop, calls=%fused_computation.102 | loop fusion | flops 1916928 | bytes 589824 | tf_op jit(solution)/shard_map/convert.28
  2.6 1.4 %copy.24 = bf16[1,2,384,384]{2,3,1,0:T(8,128)(2,1)S(1)} copy(bf16[1,2,384,384]{3,2,1,0:T(8,128)(2,1)} %param.8) | data formatting | bytes 1179648 | tf_op args[0]
  4.6 0.8 %convolution_bitcast_fusion.2 = f32[2,2,384,384]{2,3,0,1:T(8,128)S(1)} fusion(bf16[1,384,384]{1,2,0:T(8,128)(2,1)S(1)} %get-tuple-element.10, bf16[1,384,384]{1,2,0:T(8,128)(2,1)S(1)} %get-tuple-element.9, bf16[1,384,384]{2,1,0:T(8,128)(2,1)S(1)} %get-tuple-element.14, bf16[1,384,384]{2,1,0:T(8,128)(2,1)S(1)} %get-tuple-element.15), kind=kOutput, calls=%fused_computation.18 | convolution fusion | flops 455344128 | bytes 3538944 | tf_op jit(solution)/shard_map/aij,bjk->abik/dot_general | solution.py:101
  7.4 0.8 %convolution_bitcast_fusion.1 = f32[2,2,384,384]{2,3,1,0:T(8,128)S(1)} fusion(bf16[1,384,384]{1,2,0:T(8,128)(2,1)S(1)} %fusion.81, bf16[1,384,384]{1,2,0:T(8,128)(2,1)S(1)} %fusion.80, bf16[1,384,384]{2,1,0:T(8,128)(2,1)S(1)} %get-tuple-element.14, bf16[1,384,384]{2,1,0:T(8,128)(2,1)S(1)} %get-tuple-element.15), kind=kOutput, calls=%fused_computation.17 | convolution fusion | flops 455344128 | bytes 3538944 | tf_op jit(solution)/shard_map/bij,ajk->abik/dot_general | solution.py:105
  8.4 0.8 %fusion.28 = bf16[2,384,6,128]{3,1,2,0:T(8,128)(2,1)S(1)} fusion(bf16[1,384,384]{1,2,0:T(8,128)(2,1)S(1)} %get-tuple-element.8, bf16[1,384,384]{1,2,0:T(8,128)(2,1)S(1)} %get-tuple-element.7, s32[6,128]{1,0:T(8,128)S(1)} %iota_add_fusion), kind=kOutput, calls=%fused_computation.42 | convolution fusion | flops 454459392 | bytes 1772544 | tf_op jit(solution)/shard_map/gir,pik->pgrk/dot_general | solution.py:107
  9.2 2.0 %copy.102 = bf16[2,384,6,128]{3,2,1,0:T(8,128)(2,1)} copy(bf16[2,384,6,128]{3,1,2,0:T(8,128)(2,1)S(1)} %fusion.28) | data formatting | bytes 2359296 | tf_op jit(solution)/shard_map/gir,pik->pgrk/dot_general | solution.py:107
  11.2 2.2 %fusion.15 = f32[2,6,128]{2,0,1:T(2,128)S(1)} fusion(bf16[2,6,128,384]{2,1,3,0:T(8,128)(2,1)} %bitcast.245, s32[6,128]{1,0:T(8,128)S(1)} %iota_add_fusion.1, f32[6,128,128]{2,1,0:T(8,128)S(1)} %bitcast.246, bf16[1,6,128,128]{3,1,2,0:T(8,128)(2,1)S(1)} %fusion.33), kind=kOutput, calls=%fused_computation.28 | convolution fusion | flops 202209792 | bytes 1778688 | tf_op jit(solution)/shard_map/pgrq,gjq->pgrj/dot_general | solution.py:113
  13.4 5.1 %collective-permute-start.5 = (f32[2,6,128]{2,0,1:T(2,128)S(1)}, f32[2,6,128]{2,0,1:T(2,128)S(1)}, u32[]{:S(2)}, u32[]{:S(2)}) collective-permute-start(f32[2,6,128]{2,0,1:T(2,128)S(1)} %bitcast_subtract_fusion), channel_id=1, source_target_pairs={{0,3},{1,0},{2,1},{3,2},{4,7},{5,4},{6,5},{7,6},{8,11},{9,8},{10,9... | collective-permute-start | bytes 18440 | tf_op jit(solution)/shard_map/ppermute | solution.py:64
  18.5 1.0 %collective-permute-start.3 = (f32[2,6,128]{2,0,1:T(2,128)S(1)}, f32[2,6,128]{2,0,1:T(2,128)S(1)}, u32[]{:S(2)}, u32[]{:S(2)}) collective-permute-start(f32[2,6,128]{2,0,1:T(2,128)S(1)} %bitcast_subtract_fusion), channel_id=1, source_target_pairs={{0,1},{1,2},{2,3},{3,0},{4,5},{5,6},{6,7},{7,4},{8,9},{9,10},{10,1... | collective-permute-start | bytes 18440 | tf_op jit(solution)/shard_map/ppermute | solution.py:64
  20.3 2.5 %collective-permute-start = (bf16[2,96,384]{2,1,0:T(8,128)(2,1)}, bf16[2,96,384]{2,1,0:T(8,128)(2,1)}, u32[]{:S(2)}, u32[]{:S(2)}) collective-permute-start(bf16[2,96,384]{2,1,0:T(8,128)(2,1)} %get-tuple-element.11), channel_id=1, source_target_pairs={{0,1},{1,2},{2,3},{3,0},{4,5},{5,6},{6,7},{7,4},{8,9},{9,10},{10,1... | collective-permute-start | bytes 442376 | tf_op jit(solution)/shard_map/ppermute | solution.py:64
  22.8 0.9 %collective-permute-start.1 = (bf16[2,96,384]{2,1,0:T(8,128)(2,1)}, bf16[2,96,384]{2,1,0:T(8,128)(2,1)}, u32[]{:S(2)}, u32[]{:S(2)}) collective-permute-start(bf16[2,96,384]{2,1,0:T(8,128)(2,1)} %get-tuple-element.12), channel_id=1, source_target_pairs={{0,2},{1,3},{2,0},{3,1},{4,6},{5,7},{6,4},{7,5},{8,10},{9,11},{10,... | collective-permute-start | bytes 442376 | tf_op jit(solution)/shard_map/ppermute | solution.py:64
  23.7 1.1 %fusion.30 = bf16[2,96,6,128,1,1]{3,1,2,0,5,4:T(8,128)(2,1)} fusion(s32[6,128]{1,0:T(8,128)S(1)} %iota_add_fusion, s32[]{:T(128)S(6)} %select_n.70, bf16[1,384,384]{2,1,0:T(8,128)(2,1)S(1)} %get-tuple-element.15, bf16[1,384,384]{2,1,0:T(8,128)(2,1)S(1)} %get-tuple-element.14), kind=kOutput, calls=%fused_computation.43 | convolution fusion | flops 113983488 | bytes 887812 | tf_op jit(solution)/shard_map/aij,gjr->aigr/dot_general | solution.py:131
  25.5 1.5 %collective-permute-start.2 = (bf16[2,96,384]{2,1,0:T(8,128)(2,1)}, bf16[2,96,384]{2,1,0:T(8,128)(2,1)}, u32[]{:S(2)}, u32[]{:S(2)}) collective-permute-start(bf16[2,96,384]{2,1,0:T(8,128)(2,1)} %get-tuple-element.13), channel_id=1, source_target_pairs={{0,3},{1,0},{2,1},{3,2},{4,7},{5,4},{6,5},{7,6},{8,11},{9,8},{10,9... | collective-permute-start | bytes 442376 | tf_op jit(solution)/shard_map/ppermute | solution.py:64
  27.6 2.8 %copy.103 = bf16[6,128,4,2,128]{4,3,2,1,0:T(2,128)(2,1)} copy(bf16[6,128,4,2,128]{4,1,3,2,0:T(8,128)(2,1)S(1)} %convolution_convert_fusion.2) | data formatting | bytes 3145728
  30.4 3.8 %fusion.6 = f32[2,2,4,96,384]{4,3,0,1,2:T(8,128)S(1)} fusion(bf16[2,96,6,128,1,1]{3,1,2,0,5,4:T(8,128)(2,1)} %fusion.30, bf16[4,2,6,128,128]{3,1,0,4,2:T(2,128)(2,1)} %bitcast.244, s32[6,128]{1,0:T(8,128)S(1)} %iota_add_fusion.1), kind=kOutput, calls=%fused_computation.14 | convolution fusion | flops 1512603648 | bytes 4230144 | tf_op jit(solution)/shard_map/aigr,cbgrk->abcik/dot_general | solution.py:134
  35.2 1.2 %maximum_convert_fusion.1 = f32[4,2,96,384]{3,2,0,1:T(8,128)S(1)} fusion(bf16[1,2,96,384]{3,2,0,1:T(8,128)(2,1)} %bitcast.6, bf16[1,2,96,384]{3,2,0,1:T(8,128)(2,1)} %bitcast.4, bf16[1,2,96,384]{3,2,0,1:T(8,128)(2,1)} %bitcast.2, bf16[1,2,96,384]{3,2,0,1:T(8,128)(2,1)S(1)} %copy-done.1), kind=kLoop, calls=%fused_computation.77 | loop fusion | flops 1179648 | bytes 1769472 | tf_op jit(solution)/shard_map/convert_element_type | solution.py:140
  36.7 2.1 %collective-permute-start.6 = (bf16[2,96,384]{2,1,0:T(8,128)(2,1)S(1)}, bf16[2,96,384]{2,1,0:T(8,128)(2,1)S(1)}, u32[]{:S(2)}, u32[]{:S(2)}) collective-permute-start(bf16[2,96,384]{2,1,0:T(8,128)(2,1)S(1)} %pad_maximum_fusion.5), channel_id=1, source_target_pairs={{0,1},{1,2},{2,3},{3,0},{4,5},{5,6},{6,7},{7,4},{8,9},{9,10},{10,1... | collective-permute-start | bytes 442376 | tf_op jit(solution)/shard_map/ppermute | solution.py:180
  38.8 1.3 %collective-permute-start.10 = (bf16[1,2,384,384]{2,3,1,0:T(8,128)(2,1)S(1)}, bf16[1,2,384,384]{2,3,1,0:T(8,128)(2,1)S(1)}, u32[]{:S(2)}, u32[]{:S(2)}) collective-permute-start(bf16[1,2,384,384]{2,3,1,0:T(8,128)(2,1)S(1)} %copy.24), channel_id=1, source_target_pairs={{4,0},{8,4},{12,8},{5,1},{9,5},{13,9},{6,2},{10,6},{14,10},{7,3},{... | collective-permute-start | bytes 1769480 | tf_op jit(solution)/shard_map/ppermute | solution.py:28
  40.1 3.9 %collective-permute-start.9 = (bf16[1,2,384,384]{2,3,1,0:T(8,128)(2,1)S(1)}, bf16[1,2,384,384]{2,3,1,0:T(8,128)(2,1)}, u32[]{:S(2)}, u32[]{:S(2)}) collective-permute-start(bf16[1,2,384,384]{2,3,1,0:T(8,128)(2,1)S(1)} %copy.24), channel_id=1, source_target_pairs={{0,4},{4,8},{8,12},{1,5},{5,9},{9,13},{2,6},{6,10},{10,14},{3,7},{... | collective-permute-start | bytes 1769480 | tf_op jit(solution)/shard_map/ppermute | solution.py:26
  44.0 1.8 %collective-permute-start.8 = (bf16[2,96,384]{2,1,0:T(8,128)(2,1)S(1)}, bf16[2,96,384]{2,1,0:T(8,128)(2,1)S(1)}, u32[]{:S(2)}, u32[]{:S(2)}) collective-permute-start(bf16[2,96,384]{2,1,0:T(8,128)(2,1)S(1)} %pad_maximum_fusion.5), channel_id=1, source_target_pairs={{1,0},{2,1},{3,2},{0,3},{5,4},{6,5},{7,6},{4,7},{9,8},{10,9},{11,1... | collective-permute-start | bytes 442376 | tf_op jit(solution)/shard_map/ppermute | solution.py:182
  46.1 4.0 %collective-permute-done.8 = bf16[2,96,384]{2,1,0:T(8,128)(2,1)S(1)} collective-permute-done((bf16[2,96,384]{2,1,0:T(8,128)(2,1)S(1)}, bf16[2,96,384]{2,1,0:T(8,128)(2,1)S(1)}, u32[]{:S(2)}, u32[]{:S(2)}) %collective-permute-start.8) | collective-permute-done | bytes 147488 | tf_op jit(solution)/shard_map/ppermute | solution.py:182
  50.1 3.9 %collective-permute-done.7 = bf16[2,96,384]{2,1,0:T(8,128)(2,1)S(1)} collective-permute-done((bf16[2,96,384]{2,1,0:T(8,128)(2,1)S(1)}, bf16[2,96,384]{2,1,0:T(8,128)(2,1)S(1)}, u32[]{:S(2)}, u32[]{:S(2)}) %collective-permute-start.7) | collective-permute-done | bytes 147488 | tf_op jit(solution)/shard_map/ppermute | solution.py:180
  55.3 1.3 %maximum_convert_fusion = f32[3,2,384,384]{2,3,1,0:T(8,128)S(1)} fusion(bf16[1,2,384,384]{2,3,1,0:T(8,128)(2,1)S(1)} %collective-permute-done.10, bf16[1,2,384,384]{2,3,1,0:T(8,128)(2,1)S(1)} %copy.24, bf16[1,2,384,384]{2,3,1,0:T(8,128)(2,1)} %collective-permute-done.9), kind=kLoop, calls=%fused_computation.13 | loop fusion | flops 2654208 | bytes 5308416 | tf_op jit(solution)/shard_map/convert_element_type | solution.py:52
  57.8 1.4 %copy.40 = f32[1,2,384,384]{3,2,1,0:T(8,128)} copy(f32[1,2,384,384]{2,3,1,0:T(8,128)S(1)} %fusion.19) | data formatting | bytes 2359296 | tf_op jit(solution)/shard_map/sub | solution.py:60
  (63 shorter events, 8.7 us)
Async XLA Ops:
  0.0 4.0 %copy-start = (bf16[1,2,384,384]{3,2,1,0:T(8,128)(2,1)S(1)}, bf16[1,2,384,384]{3,2,1,0:T(8,128)(2,1)}, u32[]{:S(2)}) copy-start(bf16[1,2,384,384]{3,2,1,0:T(8,128)(2,1)} %param.9) | copy-start | bytes 1769476
  5.4 0.7 %copy-start.6 = (s32[1,6]{1,0:T(1,128)S(1)}, s32[1,6]{1,0:T(1,128)}, u32[]{:S(2)}) copy-start(s32[1,6]{1,0:T(1,128)} %param.12) | copy-start | bytes 76
  5.5 0.7 %copy-start.7 = (s32[1,6]{1,0:T(1,128)S(1)}, s32[1,6]{1,0:T(1,128)}, u32[]{:S(2)}) copy-start(s32[1,6]{1,0:T(1,128)} %param.13) | copy-start | bytes 76
  5.5 1.1 %copy-start.2 = (bf16[16,128,128]{2,1,0:T(8,128)(2,1)S(1)}, bf16[16,128,128]{2,1,0:T(8,128)(2,1)}, u32[]{:S(2)}) copy-start(bf16[16,128,128]{2,1,0:T(8,128)(2,1)} %param.15) | copy-start | bytes 1572868
  5.5 1.0 %copy-start.5 = (s32[1,6]{1,0:T(1,128)S(1)}, s32[1,6]{1,0:T(1,128)}, u32[]{:S(2)}) copy-start(s32[1,6]{1,0:T(1,128)} %param.11) | copy-start | bytes 76
  5.6 1.4 %copy-start.3 = (bf16[16,128,128]{2,1,0:T(8,128)(2,1)S(1)}, bf16[16,128,128]{2,1,0:T(8,128)(2,1)}, u32[]{:S(2)}) copy-start(bf16[16,128,128]{2,1,0:T(8,128)(2,1)} %param.14) | copy-start | bytes 1572868
  11.2 2.2 %copy-start.4 = (f32[1,1,2,6,128]{4,2,3,1,0:T(2,128)S(1)}, f32[1,1,2,6,128]{4,2,3,1,0:T(2,128)}, u32[]{:S(2)}) copy-start(f32[1,1,2,6,128]{4,2,3,1,0:T(2,128)} %param.10) | copy-start | bytes 18436
  13.4 12.1 %collective-permute-start.5 = (f32[2,6,128]{2,0,1:T(2,128)S(1)}, f32[2,6,128]{2,0,1:T(2,128)S(1)}, u32[]{:S(2)}, u32[]{:S(2)}) collective-permute-start(f32[2,6,128]{2,0,1:T(2,128)S(1)} %bitcast_subtract_fusion), channel_id=1, source_target_pairs={{0,3},{1,0},{2,1},{3,2},{4,7},{5,4},{6,5},{7,6},{8,11},{9,8},{10,9... | collective-permute-start | bytes 18440 | tf_op jit(solution)/shard_map/ppermute | solution.py:64
  18.5 8.4 %collective-permute-start.4 = (f32[2,6,128]{2,0,1:T(2,128)S(1)}, f32[2,6,128]{2,0,1:T(2,128)S(1)}, u32[]{:S(2)}, u32[]{:S(2)}) collective-permute-start(f32[2,6,128]{2,0,1:T(2,128)S(1)} %bitcast_subtract_fusion), channel_id=1, source_target_pairs={{0,2},{1,3},{2,0},{3,1},{4,6},{5,7},{6,4},{7,5},{8,10},{9,11},{10,... | collective-permute-start | bytes 18440 | tf_op jit(solution)/shard_map/ppermute | solution.py:64
  18.5 8.4 %collective-permute-start.3 = (f32[2,6,128]{2,0,1:T(2,128)S(1)}, f32[2,6,128]{2,0,1:T(2,128)S(1)}, u32[]{:S(2)}, u32[]{:S(2)}) collective-permute-start(f32[2,6,128]{2,0,1:T(2,128)S(1)} %bitcast_subtract_fusion), channel_id=1, source_target_pairs={{0,1},{1,2},{2,3},{3,0},{4,5},{5,6},{6,7},{7,4},{8,9},{9,10},{10,1... | collective-permute-start | bytes 18440 | tf_op jit(solution)/shard_map/ppermute | solution.py:64
  20.3 14.8 %collective-permute-start = (bf16[2,96,384]{2,1,0:T(8,128)(2,1)}, bf16[2,96,384]{2,1,0:T(8,128)(2,1)}, u32[]{:S(2)}, u32[]{:S(2)}) collective-permute-start(bf16[2,96,384]{2,1,0:T(8,128)(2,1)} %get-tuple-element.11), channel_id=1, source_target_pairs={{0,1},{1,2},{2,3},{3,0},{4,5},{5,6},{6,7},{7,4},{8,9},{9,10},{10,1... | collective-permute-start | bytes 442376 | tf_op jit(solution)/shard_map/ppermute | solution.py:64
  22.8 12.4 %collective-permute-start.1 = (bf16[2,96,384]{2,1,0:T(8,128)(2,1)}, bf16[2,96,384]{2,1,0:T(8,128)(2,1)}, u32[]{:S(2)}, u32[]{:S(2)}) collective-permute-start(bf16[2,96,384]{2,1,0:T(8,128)(2,1)} %get-tuple-element.12), channel_id=1, source_target_pairs={{0,2},{1,3},{2,0},{3,1},{4,6},{5,7},{6,4},{7,5},{8,10},{9,11},{10,... | collective-permute-start | bytes 442376 | tf_op jit(solution)/shard_map/ppermute | solution.py:64
  25.5 9.7 %collective-permute-start.2 = (bf16[2,96,384]{2,1,0:T(8,128)(2,1)}, bf16[2,96,384]{2,1,0:T(8,128)(2,1)}, u32[]{:S(2)}, u32[]{:S(2)}) collective-permute-start(bf16[2,96,384]{2,1,0:T(8,128)(2,1)} %get-tuple-element.13), channel_id=1, source_target_pairs={{0,3},{1,0},{2,1},{3,2},{4,7},{5,4},{6,5},{7,6},{8,11},{9,8},{10,9... | collective-permute-start | bytes 442376 | tf_op jit(solution)/shard_map/ppermute | solution.py:64
  34.3 0.9 %copy-start.1 = (bf16[1,2,96,384]{3,2,0,1:T(8,128)(2,1)S(1)}, bf16[1,2,96,384]{3,2,0,1:T(8,128)(2,1)}, u32[]{:S(2)}) copy-start(bf16[1,2,96,384]{3,2,0,1:T(8,128)(2,1)} %constant_dynamic-slice_fusion) | copy-start | bytes 442372
  36.7 9.1 %collective-permute-start.6 = (bf16[2,96,384]{2,1,0:T(8,128)(2,1)S(1)}, bf16[2,96,384]{2,1,0:T(8,128)(2,1)S(1)}, u32[]{:S(2)}, u32[]{:S(2)}) collective-permute-start(bf16[2,96,384]{2,1,0:T(8,128)(2,1)S(1)} %pad_maximum_fusion.5), channel_id=1, source_target_pairs={{0,1},{1,2},{2,3},{3,0},{4,5},{5,6},{6,7},{7,4},{8,9},{9,10},{10,1... | collective-permute-start | bytes 442376 | tf_op jit(solution)/shard_map/ppermute | solution.py:180
  38.8 16.5 %collective-permute-start.10 = (bf16[1,2,384,384]{2,3,1,0:T(8,128)(2,1)S(1)}, bf16[1,2,384,384]{2,3,1,0:T(8,128)(2,1)S(1)}, u32[]{:S(2)}, u32[]{:S(2)}) collective-permute-start(bf16[1,2,384,384]{2,3,1,0:T(8,128)(2,1)S(1)} %copy.24), channel_id=1, source_target_pairs={{4,0},{8,4},{12,8},{5,1},{9,5},{13,9},{6,2},{10,6},{14,10},{7,3},{... | collective-permute-start | bytes 1769480 | tf_op jit(solution)/shard_map/ppermute | solution.py:28
  40.1 15.2 %collective-permute-start.9 = (bf16[1,2,384,384]{2,3,1,0:T(8,128)(2,1)S(1)}, bf16[1,2,384,384]{2,3,1,0:T(8,128)(2,1)}, u32[]{:S(2)}, u32[]{:S(2)}) collective-permute-start(bf16[1,2,384,384]{2,3,1,0:T(8,128)(2,1)S(1)} %copy.24), channel_id=1, source_target_pairs={{0,4},{4,8},{8,12},{1,5},{5,9},{9,13},{2,6},{6,10},{10,14},{3,7},{... | collective-permute-start | bytes 1769480 | tf_op jit(solution)/shard_map/ppermute | solution.py:26
  44.0 6.1 %collective-permute-start.8 = (bf16[2,96,384]{2,1,0:T(8,128)(2,1)S(1)}, bf16[2,96,384]{2,1,0:T(8,128)(2,1)S(1)}, u32[]{:S(2)}, u32[]{:S(2)}) collective-permute-start(bf16[2,96,384]{2,1,0:T(8,128)(2,1)S(1)} %pad_maximum_fusion.5), channel_id=1, source_target_pairs={{1,0},{2,1},{3,2},{0,3},{5,4},{6,5},{7,6},{4,7},{9,8},{10,9},{11,1... | collective-permute-start | bytes 442376 | tf_op jit(solution)/shard_map/ppermute | solution.py:182
  45.8 8.2 %collective-permute-start.7 = (bf16[2,96,384]{2,1,0:T(8,128)(2,1)S(1)}, bf16[2,96,384]{2,1,0:T(8,128)(2,1)S(1)}, u32[]{:S(2)}, u32[]{:S(2)}) collective-permute-start(bf16[2,96,384]{2,1,0:T(8,128)(2,1)S(1)} %collective-permute-done.6), channel_id=1, source_target_pairs={{0,1},{1,2},{2,3},{3,0},{4,5},{5,6},{6,7},{7,4},{8,9},{9,10},{10,1... | collective-permute-start | bytes 442376 | tf_op jit(solution)/shard_map/ppermute | solution.py:180
